TPU v7x, 32 devices: a whole 2x2x4 slice. The times are simulated.
32 devices in a mesh: dp: 4 (over z), ctx: 8 (over y, x, core).
Axes of the slice: x: 2, y: 2, z: 4, core: 2. Of those that a mesh axis runs over, the one named last changes fastest.
Arguments:
- tokens: bfloat16 [4, 1024, 6144], P('dp', 'ctx'), may hold values from -0.1875 to 0.1875
- cotangent: bfloat16 [4, 1024, 6144], P('dp', 'ctx'), may hold values from -6 to 6
- w_router: float32 [6144], replicated, may hold values from -2 to 2
- w_query: bfloat16 [6144, 4096], P(None, 'ctx'), may hold values from -0.078125 to 0.078125
- w_key: bfloat16 [6144, 4096], P(None, 'ctx'), may hold values from -0.078125 to 0.078125
- w_value: bfloat16 [6144, 4096], P(None, 'ctx'), may hold values from -0.078125 to 0.078125
- w_out: bfloat16 [4096, 6144], P('ctx'), may hold values from -0.09375 to 0.09375
- chosen: int32 [4, 160], P('dp', 'ctx'), may hold values from -1 to 1023, as said below
- counts: int32 [4, 8], P('dp', 'ctx'), may hold values from 12 to 20, as said below
Outputs:
- layer_out: bfloat16 [4, 1024, 6144], P('dp', 'ctx')
- grad_query: bfloat16 [6144, 4096], P('dp', 'ctx')
- grad_key: bfloat16 [6144, 4096], P('dp', 'ctx')
- grad_value: bfloat16 [6144, 4096], P('dp', 'ctx')
- grad_out: bfloat16 [4096, 6144], P('ctx', 'dp')
- grad_router: float32 [6144], replicated
Inputs may be any that keep to these rules, and one draw needn't show every extreme that they name: `chosen`: for every sequence b and device block c, the first counts[b, c] of the block's slots c * 20 to (c + 1) * 20 - 1 hold increasing positions of that device's tokens, c * 128 to (c + 1) * 128 - 1; the other slots hold -1. In every sequence the counts add up to 128, and some device's block has exactly 20 used slots.
All inputs are finite; a program needn't handle non-finite values.
Results may differ from a plain program's by a relative error of at most 0.018.
Values may be sent and summed in bfloat16 or wider, within the bound.
No kernel may reach another device: no remote copies, remote signals or barrier semaphores. Data moves between devices by JAX's collectives and lax.ppermute only.
A program may use at most 128 MiB of HBM per device.

v0:
```python
import math
import jax
import jax.numpy as jnp
from jax import lax
from jax.sharding import PartitionSpec as P

HDIM = 128
HIGHEST_PRECISION = lax.Precision.HIGHEST
ROW_CONTRACT = (((0,), (0,)), ((), ()))
COLUMN_CONTRACT = (((1,), (1,)), ((), ()))


def head_norm(values, width):
    shaped = values.reshape(values.shape[0], -1, width)
    inverse = lax.rsqrt(jnp.mean(shaped * shaped, axis=-1, keepdims=True) + 1e-06)
    return (shaped * inverse, inverse)


def norm_back(grad_hat, normal, inverse):
    return inverse * (grad_hat - normal * jnp.mean(grad_hat * normal, axis=-1, keepdims=True))


def rounded_term(part):
    return lax.optimization_barrier(part.astype(jnp.bfloat16)).astype(jnp.float32)


def body(tokens, cotangent, w_router, w_query, w_key, w_value, w_out, chosen, counts):
    length = tokens.shape[1]
    capacity = chosen.shape[1]
    inner = w_query.shape[1]
    heads_here = inner // HDIM
    scale = 1.0 / math.sqrt(HDIM)
    offset = lax.axis_index("ctx") * length
    slot_ids = lax.broadcasted_iota(jnp.int32, (capacity,), 0)
    local = chosen[0] - offset
    present = (slot_ids < counts[0, 0]) & (local >= 0) & (local < length)
    columns = lax.broadcasted_iota(jnp.int32, (capacity, length), 1)
    onehot = ((local[:, None] == columns) & present[:, None]).astype(jnp.bfloat16)
    rows = jnp.dot(onehot, tokens[0], preferred_element_type=jnp.float32)
    rows_back = jnp.dot(onehot, cotangent[0], preferred_element_type=jnp.float32)
    logits = jnp.dot(rows, w_router, precision=HIGHEST_PRECISION)
    weights = jax.nn.sigmoid(logits)
    normed = (rows * lax.rsqrt(jnp.mean(rows * rows, axis=-1, keepdims=True) + 1e-05)).astype(
        jnp.bfloat16
    )
    delta = (weights[:, None] * rows_back).astype(jnp.bfloat16)
    all_normed, all_delta, all_present = (
        lax.all_gather(normed, "ctx", axis=0, tiled=True),
        lax.all_gather(delta, "ctx", axis=0, tiled=True),
        lax.all_gather(present.astype(jnp.bfloat16), "ctx", axis=0, tiled=True),
    )
    slots = all_normed.shape[0]
    query_raw = jnp.dot(all_normed, w_query, preferred_element_type=jnp.float32)
    key_raw = jnp.dot(all_normed, w_key, preferred_element_type=jnp.float32)
    value_raw = jnp.dot(all_normed, w_value, preferred_element_type=jnp.float32)
    query_hat, query_scale = head_norm(query_raw, HDIM)
    key_hat, key_scale = head_norm(key_raw, HDIM)
    query_b = query_hat.astype(jnp.bfloat16)
    key_b = key_hat.astype(jnp.bfloat16)
    value_b = value_raw.reshape(slots, heads_here, HDIM).astype(jnp.bfloat16)
    current = lax.broadcasted_iota(jnp.int32, (slots, slots), 0)
    earlier = lax.broadcasted_iota(jnp.int32, (slots, slots), 1)
    allowed = (earlier <= current) & ((all_present[None, :] > 0.5) | (earlier == current))
    scores = jnp.einsum("ihd,jhd->hij", query_b, key_b, preferred_element_type=jnp.float32) * scale
    exponent = jnp.where(allowed[None], jnp.exp(scores), 0.0)
    attend = exponent / jnp.sum(exponent, axis=-1, keepdims=True)
    attend_b = attend.astype(jnp.bfloat16)
    mixed = jnp.einsum("hij,jhd->ihd", attend_b, value_b, preferred_element_type=jnp.float32)
    mixed = mixed.astype(jnp.bfloat16).reshape(slots, inner)
    update = lax.psum_scatter(
        rounded_term(jnp.dot(mixed, w_out, preferred_element_type=jnp.float32)).astype(
            jnp.bfloat16
        ),
        "ctx",
        scatter_dimension=0,
        tiled=True,
    ).astype(jnp.float32)
    scaled = weights[:, None] * update
    spread = jnp.dot(onehot.astype(jnp.float32).T, scaled, precision=HIGHEST_PRECISION)
    layer_out = (tokens[0].astype(jnp.float32) + spread).astype(jnp.bfloat16)[None]
    gate_back = jnp.sum(rows_back * update, axis=-1) * weights * (1.0 - weights)
    router_part = jnp.dot(gate_back, rows, precision=HIGHEST_PRECISION)
    grad_router = lax.psum(router_part, ("dp", "ctx"))
    out_term = rounded_term(
        lax.dot_general(mixed, all_delta, ROW_CONTRACT, preferred_element_type=jnp.float32)
    )
    mixed_back = lax.dot_general(
        all_delta, w_out, COLUMN_CONTRACT, preferred_element_type=jnp.float32
    )
    mixed_back = mixed_back.astype(jnp.bfloat16).reshape(slots, heads_here, HDIM)
    attend_back = jnp.einsum(
        "ihd,jhd->hij", mixed_back, value_b, preferred_element_type=jnp.float32
    )
    inner_sum = jnp.sum(attend * attend_back, axis=-1, keepdims=True)
    scores_back = (attend * (attend_back - inner_sum) * scale).astype(jnp.bfloat16)
    value_back = jnp.einsum(
        "hij,ihd->jhd", attend_b, mixed_back, preferred_element_type=jnp.float32
    )
    value_back = value_back.astype(jnp.bfloat16).reshape(slots, inner)
    qhat_back = jnp.einsum("hij,jhd->ihd", scores_back, key_b, preferred_element_type=jnp.float32)
    khat_back = jnp.einsum("hij,ihd->jhd", scores_back, query_b, preferred_element_type=jnp.float32)
    query_back = (
        norm_back(qhat_back, query_hat, query_scale).astype(jnp.bfloat16).reshape(slots, inner)
    )
    key_back = norm_back(khat_back, key_hat, key_scale).astype(jnp.bfloat16).reshape(slots, inner)
    query_term = rounded_term(
        lax.dot_general(all_normed, query_back, ROW_CONTRACT, preferred_element_type=jnp.float32)
    )
    key_term = rounded_term(
        lax.dot_general(all_normed, key_back, ROW_CONTRACT, preferred_element_type=jnp.float32)
    )
    value_term = rounded_term(
        lax.dot_general(all_normed, value_back, ROW_CONTRACT, preferred_element_type=jnp.float32)
    )
    grad_query, grad_key, grad_value, grad_out = (
        lax.psum_scatter(
            query_term.astype(jnp.bfloat16), "dp", scatter_dimension=0, tiled=True
        ).astype(jnp.float32),
        lax.psum_scatter(
            key_term.astype(jnp.bfloat16), "dp", scatter_dimension=0, tiled=True
        ).astype(jnp.float32),
        lax.psum_scatter(
            value_term.astype(jnp.bfloat16), "dp", scatter_dimension=0, tiled=True
        ).astype(jnp.float32),
        lax.psum_scatter(
            out_term.astype(jnp.bfloat16), "dp", scatter_dimension=1, tiled=True
        ).astype(jnp.float32),
    )
    return (
        layer_out,
        grad_query.astype(jnp.bfloat16),
        grad_key.astype(jnp.bfloat16),
        grad_value.astype(jnp.bfloat16),
        grad_out.astype(jnp.bfloat16),
        grad_router,
    )


def solution(mesh):
    in_specs = (
        P("dp", "ctx", None),
        P("dp", "ctx", None),
        P(),
        P(None, "ctx"),
        P(None, "ctx"),
        P(None, "ctx"),
        P("ctx", None),
        P("dp", "ctx"),
        P("dp", "ctx"),
    )
    out_specs = (
        P("dp", "ctx", None),
        P("dp", "ctx"),
        P("dp", "ctx"),
        P("dp", "ctx"),
        P("ctx", "dp"),
        P(),
    )
    return jax.shard_map(body, mesh=mesh, in_specs=in_specs, out_specs=out_specs, check_vma=False)
```

profile of v0, /device:TPU:0, one launch (start us, length us, event | category | flops | bytes accessed | tf_op | source)
XLA Modules:
  0.0 630.2 jit_solution(3186163892697100419)
XLA Ops:
  8.0 0.7 fusion.88
  8.7 1.9 multiply_reduce_fusion.1
  10.6 0.9 fusion.31
  11.6 0.7 fusion.89
  13.1 15.3 %all-reduce = bf16[160]{0:T(256)(128)(2,1)S(1)} all-reduce(bf16[160]{0:T(256)(128)(2,1)S(1)} %dynamic-update-slice), channel_id=1, replica_groups=mesh['dp'=4,'ctx'=8] {'ctx'}, use_global_device_ids=true, to_apply=%add | all-reduce | flops 160 | bytes 640
  28.4 0.7 fusion.54
  29.2 14.3 %all-gather.5.cloned.1.call-done = bf16[8,20,6144]{2,1,0:T(8,128)(2,1)} async-done(((bf16[1,20,6144]{2,1,0:T(8,128)(2,1)}), bf16[8,20,6144]{2,1,0:T(8,128)(2,1)}) %all-gather.5.cloned.1.call-update) | async-done | bytes 1966096 | tf_op jit(solution)/shard_map/all_gather | solution.py:48
  43.4 2.6 reshape.127
  46.0 4.8 fusion.16
  50.8 4.8 fusion.103
  55.7 1.9 fusion.102
  57.6 1.8 reshape.116
  59.4 1.9 multiply_reduce_fusion.5
  61.3 1.0 copy.67
  62.2 1.8 reshape.117
  64.0 1.9 multiply_reduce_fusion.4
  65.9 1.0 copy.69
  66.9 2.4 fusion.28
  69.2 1.5 fusion.14
  70.8 0.6 copy-done.7
  71.4 5.4 convolution_convert_fusion.4
  76.8 30.2 %fusion = bf16[24,6144]{1,0:T(8,128)(2,1)} fusion(bf16[160,6144]{1,0:T(8,128)(2,1)} %convolution_convert_fusion.4), kind=kCustom, calls=%all-reduce-scatter | all-reduce-scatter fusion | flops 1179649 | bytes 2261504
  106.9 2.0 collective-permute-start
  108.9 1.5 slice
  110.5 3.2 collective-permute-start.1
  113.7 2.3 fusion.21
  116.6 9.6 %concatenate = bf16[52,6144]{1,0:T(8,128)(2,1)} concatenate(bf16[4,6144]{1,0:T(4,128)(2,1)} %collective-permute-done.1, bf16[24,6144]{1,0:T(8,128)(2,1)} %collective-permute-done, bf16[24,6144]{1,0:T(8,128)(2,1)} %fusion), dimensions={0} | concatenate | bytes 1277952
  126.2 2.8 fusion.26
  129.1 30.2 %all-gather.7.cloned.1.call-done = bf16[8,20,6144]{2,1,0:T(8,128)(2,1)} async-done(((bf16[1,20,6144]{2,1,0:T(8,128)(2,1)}), bf16[8,20,6144]{2,1,0:T(8,128)(2,1)}) %all-gather.7.cloned.1.call-update) | async-done | bytes 1966096 | tf_op jit(solution)/shard_map/all_gather | solution.py:49
  159.3 4.0 reshape.129
  163.3 6.0 convolution_convert_fusion
  169.6 5.8 fusion.17
  175.4 0.7 copy-done.10
  176.1 1.1 fusion.48
  177.2 2.6 multiply_reduce_fusion.3
  179.8 5.7 convolution_convert_fusion.3
  185.6 2.4 multiply_reduce_fusion.2
  188.0 5.6 convolution_convert_fusion.2
  193.6 0.8 copy-done.11
  194.7 4.4 convolution_convert_fusion.1
  199.2 1.0 copy-done.3
  200.2 0.4 fusion.77
  200.6 47.0 %psum.7 = f32[6144]{0:T(1024)} all-reduce(f32[6144]{0:T(1024)S(1)} %bitcast.169), channel_id=1, replica_groups=mesh['dp'=4,'ctx'=8] {'dp','ctx'}, use_global_device_ids=true, to_apply=%region_13.14 | all-reduce | flops 6144 | bytes 49152 | tf_op jit(solution)/shard_map/psum | solution.py:83
  247.6 4.4 fusion.3
  252.0 29.3 %reduce-scatter.13.cloned.1.call-done = bf16[512,1536]{1,0:T(8,128)(2,1)} async-done(((bf16[512,6144]{1,0:T(8,128)(2,1)}), bf16[512,1536]{1,0:T(8,128)(2,1)}) %reduce-scatter.13.cloned.1.call-update) | async-done | bytes 1572880 | tf_op jit(solution)/shard_map/reduce_scatter | solution.py:125
  281.3 114.0 %reduce-scatter.7.cloned.1.call-done = bf16[1536,512]{1,0:T(8,128)(2,1)} async-done(((bf16[6144,512]{1,0:T(8,128)(2,1)}), bf16[1536,512]{1,0:T(8,128)(2,1)}) %reduce-scatter.7.cloned.1.call-update) | async-done | bytes 1572880 | tf_op jit(solution)/shard_map/reduce_scatter | solution.py:116
  395.3 114.0 %reduce-scatter.9.cloned.1.call-done = bf16[1536,512]{1,0:T(8,128)(2,1)} async-done(((bf16[6144,512]{1,0:T(8,128)(2,1)}), bf16[1536,512]{1,0:T(8,128)(2,1)}) %reduce-scatter.9.cloned.1.call-update) | async-done | bytes 1572880 | tf_op jit(solution)/shard_map/reduce_scatter | solution.py:119
  509.3 114.0 %reduce-scatter.11.cloned.1.call-done = bf16[1536,512]{1,0:T(8,128)(2,1)} async-done(((bf16[6144,512]{1,0:T(8,128)(2,1)}), bf16[1536,512]{1,0:T(8,128)(2,1)}) %reduce-scatter.11.cloned.1.call-update) | async-done | bytes 1572880 | tf_op jit(solution)/shard_map/reduce_scatter | solution.py:122
  (61 shorter events, 1.1 us)
Async XLA Ops:
  7.2 119.0 %copy-start = (bf16[1,128,6144]{2,1,0:T(8,128)(2,1)S(1)}, bf16[1,128,6144]{2,1,0:T(8,128)(2,1)}, u32[]{:S(2)}) copy-start(bf16[1,128,6144]{2,1,0:T(8,128)(2,1)} %param.10) | copy-start | bytes 4718596
  7.2 4.4 copy-start.18
  7.2 36.2 %all-gather.5.cloned.1.call-start = ((), (), s32[]{:S(2)}) async-start(), calls=%async_computation.8 | async-start | bytes 2654208 | tf_op jit(solution)/shard_map/all_gather | solution.py:48
  8.7 20.5 %copy-start.12 = (pred[20]{0:T(512)(128)(4,1)}, pred[20]{0:T(512)(128)(4,1)S(1)}, u32[]{:S(2)}) copy-start(pred[20]{0:T(512)(128)(4,1)S(1)} %get-tuple-element.7) | copy-start | bytes 64
  8.7 20.5 %copy-start.14 = (s32[20]{0:T(128)}, s32[20]{0:T(128)S(1)}, u32[]{:S(2)}) copy-start(s32[20]{0:T(128)S(1)} %get-tuple-element.8) | copy-start | bytes 244
  10.6 18.6 %copy-start.2 = (f32[20,6144]{1,0:T(8,128)}, f32[20,6144]{1,0:T(8,128)S(1)}, u32[]{:S(2)}) copy-start(f32[20,6144]{1,0:T(8,128)S(1)} %get-tuple-element.14) | copy-start | bytes 1474564
  11.5 147.8 %all-gather.7.cloned.1.call-start = ((), (), s32[]{:S(2)}) async-start(), calls=%async_computation.9 | async-start | bytes 2654208 | tf_op jit(solution)/shard_map/all_gather | solution.py:49
  46.0 9.6 %slice-start = ((s8[6291456]{0:T(1024)(128)(4,1)}), s8[4194304]{0:T(1024)(128)(4,1)S(1)}, s32[]{:S(2)}) async-start(s8[6291456]{0:T(1024)(128)(4,1)} %bitcast.167), calls=%async_computation.10 | async-start | bytes 8388608
  50.8 4.8 slice-start.1
  70.7 0.7 copy-start.7
  76.8 49.5 %copy-start.13 = (pred[20]{0:T(512)(128)(4,1)S(1)}, pred[20]{0:T(512)(128)(4,1)}, u32[]{:S(2)}) copy-start(pred[20]{0:T(512)(128)(4,1)} %copy-done.12) | copy-start | bytes 64
  76.8 49.5 %copy-start.15 = (s32[20]{0:T(128)S(1)}, s32[20]{0:T(128)}, u32[]{:S(2)}) copy-start(s32[20]{0:T(128)} %copy-done.14) | copy-start | bytes 244
  106.9 9.7 %collective-permute-start = (bf16[24,6144]{1,0:T(8,128)(2,1)}, bf16[24,6144]{1,0:T(8,128)(2,1)}, u32[]{:S(2)}, u32[]{:S(2)}) collective-permute-start(bf16[24,6144]{1,0:T(8,128)(2,1)} %fusion), channel_id=1, source_target_pairs={{0,1},{1,2},{2,3},{3,4},{4,5},{5,6},{6,7},{8,9},{9,10},{10,11},{11... | collective-permute-start | bytes 884744
  110.5 6.2 collective-permute-start.1
  129.0 34.3 %copy-start.8 = (bf16[4,20,8,128]{3,2,1,0:T(8,128)(2,1)S(1)}, bf16[4,20,8,128]{3,2,1,0:T(8,128)(2,1)}, u32[]{:S(2)}) copy-start(bf16[4,20,8,128]{3,2,1,0:T(8,128)(2,1)} %copy-done.7) | copy-start | bytes 491524
  129.1 152.3 %reduce-scatter.13.cloned.1.call-start = ((), (), s32[]{:S(2)}) async-start(), calls=%async_computation.7 | async-start | bytes 7864320 | tf_op jit(solution)/shard_map/reduce_scatter | solution.py:125
  169.4 6.8 %copy-start.9 = (bf16[20,4,8,128]{3,2,1,0:T(8,128)(2,1)S(1)}, bf16[20,4,8,128]{3,2,1,0:T(8,128)(2,1)}, u32[]{:S(2)}) copy-start(bf16[20,4,8,128]{3,2,1,0:T(8,128)(2,1)} %fusion.16) | copy-start | bytes 491524
  169.4 7.8 %copy-start.4 = (f32[160,512]{1,0:T(8,128)S(1)}, f32[160,512]{1,0:T(8,128)}, u32[]{:S(2)}) copy-start(f32[160,512]{1,0:T(8,128)} %fusion.103) | copy-start | bytes 983044
  169.4 7.8 %copy-start.5 = (f32[160,512]{1,0:T(8,128)S(1)}, f32[160,512]{1,0:T(8,128)}, u32[]{:S(2)}) copy-start(f32[160,512]{1,0:T(8,128)} %fusion.102) | copy-start | bytes 983044
  169.4 7.8 %copy-start.6 = (f32[4,160,160]{1,2,0:T(8,128)S(1)}, f32[4,160,160]{1,2,0:T(8,128)}, u32[]{:S(2)}) copy-start(f32[4,160,160]{1,2,0:T(8,128)} %fusion.28) | copy-start | bytes 1228804
  169.4 225.9 %reduce-scatter.7.cloned.1.call-start = ((), (), s32[]{:S(2)}) async-start(), calls=%async_computation.4 | async-start | bytes 7864320 | tf_op jit(solution)/shard_map/reduce_scatter | solution.py:116
  175.4 0.7 copy-start.10
  185.5 323.8 %reduce-scatter.9.cloned.1.call-start = ((), (), s32[]{:S(2)}) async-start(), calls=%async_computation.5 | async-start | bytes 7864320 | tf_op jit(solution)/shard_map/reduce_scatter | solution.py:119
  193.5 0.9 copy-start.11
  193.6 429.8 %reduce-scatter.11.cloned.1.call-start = ((), (), s32[]{:S(2)}) async-start(), calls=%async_computation.6 | async-start | bytes 7864320 | tf_op jit(solution)/shard_map/reduce_scatter | solution.py:122
  199.1 1.1 copy-start.3
  199.1 1.1 copy-start.16
  199.1 1.1 copy-start.17
  199.2 424.2 %copy-start.1 = (bf16[1,128,6144]{2,1,0:T(8,128)(2,1)S(1)}, bf16[1,128,6144]{2,1,0:T(8,128)(2,1)}, u32[]{:S(2)}) copy-start(bf16[1,128,6144]{2,1,0:T(8,128)(2,1)} %param.10) | copy-start | bytes 4718596
Sparse Core Ops, SparseCore 0:
  11.6 31.7 all-gather.4
  129.2 30.0 all-gather.6
  169.5 111.7 reduce-scatter.12
  284.1 111.2 reduce-scatter.6
  398.0 111.2 reduce-scatter.8
  512.1 111.2 reduce-scatter.10
where the time goes:
time: 632 us; the launch traced here: 630 us
  waiting for transfers between devices  416 us (66%)
  blocking collectives  92.5 us (15%)
  matrix products  66.3 us (10%)
  local copies, waits for them, and re-layouts  27.4 us (4%)
  between operations  16.4 us (3%)
    reduce_scatter x1, waiting for transfers between devices, body(): lax.psum_scatter(value_term.astype(jnp.bfloat16), 'dp', scatter_dimension...  114 us
    reduce_scatter x1, waiting for transfers between devices, body(): lax.psum_scatter(key_term.astype(jnp.bfloat16), 'dp', scatter_dimension=0...  114 us
    reduce_scatter x1, waiting for transfers between devices, body(): lax.psum_scatter(query_term.astype(jnp.bfloat16), 'dp', scatter_dimension...  114 us
    psum x1, blocking collectives, body(): grad_router = lax.psum(router_part, ('dp', 'ctx'))  47 us
    unnamed x2, blocking collectives  45.5 us
    all_gather x1, waiting for transfers between devices, body(): lax.all_gather(delta, 'ctx', axis=0, tiled=True)  30.2 us
    reduce_scatter x1, waiting for transfers between devices, body(): lax.psum_scatter(out_term.astype(jnp.bfloat16), 'dp', scatter_dimension=1...  29.3 us
    unnamed x49, local copies, waits for them, and re-layouts  21.9 us
  transfers between devices with their start and end apart: 8, of which 6 were waited for; matrix products, arithmetic and copies ran while one was open for 6% of the time, Pallas kernels for 0%

commit v1 on v0

--- a/solution.py
+++ b/solution.py
@@ -80,7 +80,7 @@
     layer_out = (tokens[0].astype(jnp.float32) + spread).astype(jnp.bfloat16)[None]
     gate_back = jnp.sum(rows_back * update, axis=-1) * weights * (1.0 - weights)
     router_part = jnp.dot(gate_back, rows, precision=HIGHEST_PRECISION)
-    grad_router = lax.psum(router_part, ("dp", "ctx"))
+    grad_router = jax.lax.psum(jax.lax.psum(router_part, "ctx"), "dp")
     out_term = rounded_term(
         lax.dot_general(mixed, all_delta, ROW_CONTRACT, preferred_element_type=jnp.float32)
     )

time: 632 us -> 632 us (level)
    psum x1 -> x2, blocking collectives: 47 us -> 46.6 us  [body(): grad_router = jax.lax.psum(jax.lax.psum(router_part, 'ctx'), 'dp')]
where the time goes in v1:
time: 632 us; the launch traced here: 630 us
  waiting for transfers between devices  417 us (66%)
  blocking collectives  92.1 us (15%)
  matrix products  66.3 us (10%)
  local copies, waits for them, and re-layouts  27.2 us (4%)
  between operations  16.4 us (3%)
    reduce_scatter x1, waiting for transfers between devices, body(): lax.psum_scatter(query_term.astype(jnp.bfloat16), 'dp', scatter_dimension...  114 us
    reduce_scatter x1, waiting for transfers between devices, body(): lax.psum_scatter(value_term.astype(jnp.bfloat16), 'dp', scatter_dimension...  114 us
    reduce_scatter x1, waiting for transfers between devices, body(): lax.psum_scatter(key_term.astype(jnp.bfloat16), 'dp', scatter_dimension=0...  114 us
    psum x2, blocking collectives, body(): grad_router = jax.lax.psum(jax.lax.psum(router_part, 'ctx'), 'dp')  46.6 us
    unnamed x2, blocking collectives  45.5 us
    all_gather x1, waiting for transfers between devices, body(): lax.all_gather(delta, 'ctx', axis=0, tiled=True)  30.3 us
    reduce_scatter x1, waiting for transfers between devices, body(): lax.psum_scatter(out_term.astype(jnp.bfloat16), 'dp', scatter_dimension=1...  29.7 us
    unnamed x49, local copies, waits for them, and re-layouts  21.7 us
  transfers between devices with their start and end apart: 8, of which 6 were waited for; matrix products, arithmetic and copies ran while one was open for 6% of the time, Pallas kernels for 0%

profile of v1, /device:TPU:0, one launch (start us, length us, event | category | flops | bytes accessed | tf_op | source)
XLA Modules:
  0.0 630.2 jit_solution(6419018808775178363)
XLA Ops:
  8.0 0.7 fusion.88
  8.7 1.9 multiply_reduce_fusion.1
  10.6 0.9 fusion.31
  11.6 0.6 fusion.89
  13.1 15.3 %all-reduce = bf16[160]{0:T(256)(128)(2,1)S(1)} all-reduce(bf16[160]{0:T(256)(128)(2,1)S(1)} %dynamic-update-slice), channel_id=1, replica_groups=mesh['dp'=4,'ctx'=8] {'ctx'}, use_global_device_ids=true, to_apply=%add | all-reduce | flops 160 | bytes 640
  28.4 0.7 fusion.54
  29.1 14.3 %all-gather.5.cloned.1.call-done = bf16[8,20,6144]{2,1,0:T(8,128)(2,1)} async-done(((bf16[1,20,6144]{2,1,0:T(8,128)(2,1)}), bf16[8,20,6144]{2,1,0:T(8,128)(2,1)}) %all-gather.5.cloned.1.call-update) | async-done | bytes 1966096 | tf_op jit(solution)/shard_map/all_gather | solution.py:48
  43.4 2.6 reshape.127
  46.0 4.8 fusion.16
  50.8 4.8 fusion.103
  55.7 2.0 fusion.102
  57.6 1.8 reshape.116
  59.4 1.9 multiply_reduce_fusion.5
  61.3 1.0 copy.67
  62.3 1.8 reshape.117
  64.1 1.9 multiply_reduce_fusion.4
  65.9 1.0 copy.69
  66.9 2.4 fusion.28
  69.3 1.5 fusion.14
  70.8 0.7 copy-done.7
  71.4 5.3 convolution_convert_fusion.4
  76.8 30.2 %fusion = bf16[24,6144]{1,0:T(8,128)(2,1)} fusion(bf16[160,6144]{1,0:T(8,128)(2,1)} %convolution_convert_fusion.4), kind=kCustom, calls=%all-reduce-scatter | all-reduce-scatter fusion | flops 1179649 | bytes 2261504
  107.0 2.0 collective-permute-start
  108.9 1.5 slice
  110.5 3.2 collective-permute-start.1
  113.7 2.3 fusion.21
  116.6 9.5 %concatenate = bf16[52,6144]{1,0:T(8,128)(2,1)} concatenate(bf16[4,6144]{1,0:T(4,128)(2,1)} %collective-permute-done.1, bf16[24,6144]{1,0:T(8,128)(2,1)} %collective-permute-done, bf16[24,6144]{1,0:T(8,128)(2,1)} %fusion), dimensions={0} | concatenate | bytes 1277952
  126.1 2.8 fusion.26
  129.0 30.3 %all-gather.7.cloned.1.call-done = bf16[8,20,6144]{2,1,0:T(8,128)(2,1)} async-done(((bf16[1,20,6144]{2,1,0:T(8,128)(2,1)}), bf16[8,20,6144]{2,1,0:T(8,128)(2,1)}) %all-gather.7.cloned.1.call-update) | async-done | bytes 1966096 | tf_op jit(solution)/shard_map/all_gather | solution.py:49
  159.2 4.0 reshape.129
  163.2 6.1 convolution_convert_fusion
  169.6 5.8 fusion.17
  175.4 0.7 copy-done.10
  176.0 1.1 fusion.48
  177.1 2.6 multiply_reduce_fusion.3
  179.7 5.6 convolution_convert_fusion.3
  185.5 2.4 multiply_reduce_fusion.2
  187.8 5.6 convolution_convert_fusion.2
  193.5 0.8 copy-done.11
  194.6 4.4 convolution_convert_fusion.1
  199.1 1.0 copy-done.3
  200.5 25.0 %psum.14 = f32[6144]{0:T(1024)S(1)} all-reduce(f32[6144]{0:T(1024)S(1)} %bitcast.169), channel_id=1, replica_groups=mesh['dp'=4,'ctx'=8] {'ctx'}, use_global_device_ids=true, to_apply=%region_13.14 | all-reduce | flops 6144 | bytes 49152 | tf_op jit(solution)/shard_map/psum | solution.py:83
  225.5 21.7 %psum.15 = f32[6144]{0:T(1024)} all-reduce(f32[6144]{0:T(1024)S(1)} %psum.14), channel_id=1, replica_groups=mesh['dp'=4,'ctx'=8] {'dp'}, use_global_device_ids=true, to_apply=%region_14.15 | all-reduce | flops 6144 | bytes 49152 | tf_op jit(solution)/shard_map/psum | solution.py:83
  247.2 4.4 fusion.3
  251.5 29.7 %reduce-scatter.13.cloned.1.call-done = bf16[512,1536]{1,0:T(8,128)(2,1)} async-done(((bf16[512,6144]{1,0:T(8,128)(2,1)}), bf16[512,1536]{1,0:T(8,128)(2,1)}) %reduce-scatter.13.cloned.1.call-update) | async-done | bytes 1572880 | tf_op jit(solution)/shard_map/reduce_scatter | solution.py:125
  281.3 114.0 %reduce-scatter.7.cloned.1.call-done = bf16[1536,512]{1,0:T(8,128)(2,1)} async-done(((bf16[6144,512]{1,0:T(8,128)(2,1)}), bf16[1536,512]{1,0:T(8,128)(2,1)}) %reduce-scatter.7.cloned.1.call-update) | async-done | bytes 1572880 | tf_op jit(solution)/shard_map/reduce_scatter | solution.py:116
  395.3 114.0 %reduce-scatter.9.cloned.1.call-done = bf16[1536,512]{1,0:T(8,128)(2,1)} async-done(((bf16[6144,512]{1,0:T(8,128)(2,1)}), bf16[1536,512]{1,0:T(8,128)(2,1)}) %reduce-scatter.9.cloned.1.call-update) | async-done | bytes 1572880 | tf_op jit(solution)/shard_map/reduce_scatter | solution.py:119
  509.3 114.0 %reduce-scatter.11.cloned.1.call-done = bf16[1536,512]{1,0:T(8,128)(2,1)} async-done(((bf16[6144,512]{1,0:T(8,128)(2,1)}), bf16[1536,512]{1,0:T(8,128)(2,1)}) %reduce-scatter.11.cloned.1.call-update) | async-done | bytes 1572880 | tf_op jit(solution)/shard_map/reduce_scatter | solution.py:122
  (62 shorter events, 1.5 us)
Async XLA Ops:
  7.2 118.9 %copy-start = (bf16[1,128,6144]{2,1,0:T(8,128)(2,1)S(1)}, bf16[1,128,6144]{2,1,0:T(8,128)(2,1)}, u32[]{:S(2)}) copy-start(bf16[1,128,6144]{2,1,0:T(8,128)(2,1)} %param.10) | copy-start | bytes 4718596
  7.2 4.4 copy-start.18
  7.2 36.2 %all-gather.5.cloned.1.call-start = ((), (), s32[]{:S(2)}) async-start(), calls=%async_computation.8 | async-start | bytes 2654208 | tf_op jit(solution)/shard_map/all_gather | solution.py:48
  8.7 20.4 %copy-start.12 = (pred[20]{0:T(512)(128)(4,1)}, pred[20]{0:T(512)(128)(4,1)S(1)}, u32[]{:S(2)}) copy-start(pred[20]{0:T(512)(128)(4,1)S(1)} %get-tuple-element.7) | copy-start | bytes 64
  8.7 20.4 %copy-start.14 = (s32[20]{0:T(128)}, s32[20]{0:T(128)S(1)}, u32[]{:S(2)}) copy-start(s32[20]{0:T(128)S(1)} %get-tuple-element.8) | copy-start | bytes 244
  10.6 18.5 %copy-start.2 = (f32[20,6144]{1,0:T(8,128)}, f32[20,6144]{1,0:T(8,128)S(1)}, u32[]{:S(2)}) copy-start(f32[20,6144]{1,0:T(8,128)S(1)} %get-tuple-element.14) | copy-start | bytes 1474564
  11.5 147.7 %all-gather.7.cloned.1.call-start = ((), (), s32[]{:S(2)}) async-start(), calls=%async_computation.9 | async-start | bytes 2654208 | tf_op jit(solution)/shard_map/all_gather | solution.py:49
  46.0 9.6 %slice-start = ((s8[6291456]{0:T(1024)(128)(4,1)}), s8[4194304]{0:T(1024)(128)(4,1)S(1)}, s32[]{:S(2)}) async-start(s8[6291456]{0:T(1024)(128)(4,1)} %bitcast.167), calls=%async_computation.10 | async-start | bytes 8388608
  50.8 4.8 slice-start.1
  70.8 0.7 copy-start.7
  76.8 49.3 %copy-start.13 = (pred[20]{0:T(512)(128)(4,1)S(1)}, pred[20]{0:T(512)(128)(4,1)}, u32[]{:S(2)}) copy-start(pred[20]{0:T(512)(128)(4,1)} %copy-done.12) | copy-start | bytes 64
  76.8 49.3 %copy-start.15 = (s32[20]{0:T(128)S(1)}, s32[20]{0:T(128)}, u32[]{:S(2)}) copy-start(s32[20]{0:T(128)} %copy-done.14) | copy-start | bytes 244
  107.0 9.6 %collective-permute-start = (bf16[24,6144]{1,0:T(8,128)(2,1)}, bf16[24,6144]{1,0:T(8,128)(2,1)}, u32[]{:S(2)}, u32[]{:S(2)}) collective-permute-start(bf16[24,6144]{1,0:T(8,128)(2,1)} %fusion), channel_id=1, source_target_pairs={{0,1},{1,2},{2,3},{3,4},{4,5},{5,6},{6,7},{8,9},{9,10},{10,11},{11... | collective-permute-start | bytes 884744
  110.5 6.1 collective-permute-start.1
  128.9 34.3 %copy-start.8 = (bf16[4,20,8,128]{3,2,1,0:T(8,128)(2,1)S(1)}, bf16[4,20,8,128]{3,2,1,0:T(8,128)(2,1)}, u32[]{:S(2)}) copy-start(bf16[4,20,8,128]{3,2,1,0:T(8,128)(2,1)} %copy-done.7) | copy-start | bytes 491524
  128.9 152.3 %reduce-scatter.13.cloned.1.call-start = ((), (), s32[]{:S(2)}) async-start(), calls=%async_computation.7 | async-start | bytes 7864320 | tf_op jit(solution)/shard_map/reduce_scatter | solution.py:125
  169.3 6.7 %copy-start.9 = (bf16[20,4,8,128]{3,2,1,0:T(8,128)(2,1)S(1)}, bf16[20,4,8,128]{3,2,1,0:T(8,128)(2,1)}, u32[]{:S(2)}) copy-start(bf16[20,4,8,128]{3,2,1,0:T(8,128)(2,1)} %fusion.16) | copy-start | bytes 491524
  169.3 7.8 %copy-start.4 = (f32[160,512]{1,0:T(8,128)S(1)}, f32[160,512]{1,0:T(8,128)}, u32[]{:S(2)}) copy-start(f32[160,512]{1,0:T(8,128)} %fusion.103) | copy-start | bytes 983044
  169.3 7.8 %copy-start.5 = (f32[160,512]{1,0:T(8,128)S(1)}, f32[160,512]{1,0:T(8,128)}, u32[]{:S(2)}) copy-start(f32[160,512]{1,0:T(8,128)} %fusion.102) | copy-start | bytes 983044
  169.3 7.8 %copy-start.6 = (f32[4,160,160]{1,2,0:T(8,128)S(1)}, f32[4,160,160]{1,2,0:T(8,128)}, u32[]{:S(2)}) copy-start(f32[4,160,160]{1,2,0:T(8,128)} %fusion.28) | copy-start | bytes 1228804
  169.3 226.0 %reduce-scatter.7.cloned.1.call-start = ((), (), s32[]{:S(2)}) async-start(), calls=%async_computation.4 | async-start | bytes 7864320 | tf_op jit(solution)/shard_map/reduce_scatter | solution.py:116
  175.4 0.7 copy-start.10
  185.4 323.9 %reduce-scatter.9.cloned.1.call-start = ((), (), s32[]{:S(2)}) async-start(), calls=%async_computation.5 | async-start | bytes 7864320 | tf_op jit(solution)/shard_map/reduce_scatter | solution.py:119
  193.5 0.9 copy-start.11
  193.5 429.9 %reduce-scatter.11.cloned.1.call-start = ((), (), s32[]{:S(2)}) async-start(), calls=%async_computation.6 | async-start | bytes 7864320 | tf_op jit(solution)/shard_map/reduce_scatter | solution.py:122
  199.1 1.1 copy-start.3
  199.1 1.1 copy-start.16
  199.1 1.1 copy-start.17
  199.1 424.3 %copy-start.1 = (bf16[1,128,6144]{2,1,0:T(8,128)(2,1)S(1)}, bf16[1,128,6144]{2,1,0:T(8,128)(2,1)}, u32[]{:S(2)}) copy-start(bf16[1,128,6144]{2,1,0:T(8,128)(2,1)} %param.10) | copy-start | bytes 4718596
Sparse Core Ops, SparseCore 0:
  11.6 31.7 all-gather.4
  129.0 30.1 all-gather.6
  169.4 111.7 reduce-scatter.12
  284.0 111.2 reduce-scatter.6
  398.0 111.2 reduce-scatter.8
  512.1 111.2 reduce-scatter.10
